TPU v7x, 32 devices: a whole 2x2x4 slice. The times are simulated.
32 devices in a mesh: blk: 8 (over z, y), corpus: 4 (over x, core).
Axes of the slice: x: 2, y: 2, z: 4, core: 2. Of those that a mesh axis runs over, the one named last changes fastest.
Arguments:
- queries: bfloat16 [1024, 4096], P('blk', 'corpus'), may hold values from -12 to 12
- passages: bfloat16 [1024, 4096], P('blk', 'corpus'), may hold values from -4 to 4
- table: bfloat16 [1024, 4096], P('corpus'), may hold values from -4 to 4
- neg_owner: int32 [1024, 7], P('blk'), may hold values from 0 to 3, as said below
- neg_row: int32 [1024, 7], P('blk'), may hold values from 0 to 255
- positive: int32 [1024], P('blk'), may hold values from 0 to 1023, each once
- loss_weight: float32 [1024], P('blk'), may hold values from 32 to 256
Outputs:
- losses: float32 [1024], P(('blk', 'corpus'))
- query_grad: float32 [1024, 4096], P('blk', 'corpus')
- passage_grad: float32 [1024, 4096], P('blk', 'corpus')
- table_grad: float32 [1024, 4096], P('corpus', 'blk')
Inputs may be any that keep to these rules, and one draw needn't show every extreme that they name: `neg_owner`: among the 896 references of the queries of one index of blk (aligned blocks of 128 queries), one shard is named exactly 448 times and no shard more often.
All inputs are finite; a program needn't handle non-finite values.
Results may differ from a plain program's by a relative error of at most 0.0065.
Values may be sent and summed in bfloat16 or wider, within the bound.
No kernel may reach another device: no remote copies, remote signals or barrier semaphores. Data moves between devices by JAX's collectives and lax.ppermute only.
A program may use at most 128 MiB of HBM per device.

v0:
```python
import jax
import jax.numpy as jnp
from jax import lax
from jax.sharding import PartitionSpec as P


def hi_lo(mixing):
    upper = mixing.astype(jnp.bfloat16)
    lower = (mixing - upper.astype(jnp.float32)).astype(jnp.bfloat16)
    return (upper, lower)


def per_device(queries, passages, table, neg_owner, neg_row, positive, loss_weight):
    q_rows, col_width = queries.shape
    owner_count = lax.axis_size("corpus")
    blk_count = lax.axis_size("blk")
    factor = (col_width * owner_count) ** (-0.5)
    rows_shard = table.shape[0]
    table_rows = owner_count * rows_shard
    owner_index = lax.axis_index("corpus")
    blk_index = lax.axis_index("blk")
    table_cols = lax.all_to_all(table, "corpus", split_axis=1, concat_axis=0, tiled=True)
    all_passages = lax.all_gather(passages, "blk", axis=0, tiled=True)
    all_queries = lax.all_gather(queries, "blk", axis=0, tiled=True)
    ids = neg_owner * rows_shard + neg_row
    all_ids = lax.all_gather(ids, "blk", axis=0, tiled=True)
    all_rows = all_passages.shape[0]
    logits = lax.dot_general(
        queries, all_passages, (((1,), (1,)), ((), ())), preferred_element_type=jnp.float32
    )
    table_scores = lax.dot_general(
        queries, table_cols, (((1,), (1,)), ((), ())), preferred_element_type=jnp.float32
    )
    row_iota = jnp.arange(table_rows, dtype=jnp.int32)
    picks = ids[:, :, None] == row_iota[None, None, :]
    hard_logits = jnp.sum(jnp.where(picks, table_scores[:, None, :], 0.0), axis=2)
    logits, hard_logits = lax.psum((logits, hard_logits), "corpus")
    logits = logits * factor
    hard_logits = hard_logits * factor
    row_top = jnp.maximum(jnp.max(logits, axis=1), jnp.max(hard_logits, axis=1))
    log_total = row_top + jnp.log(
        jnp.sum(jnp.exp(logits - row_top[:, None]), axis=1)
        + jnp.sum(jnp.exp(hard_logits - row_top[:, None]), axis=1)
    )
    one_hot = positive[:, None] == jnp.arange(all_rows, dtype=jnp.int32)[None, :]
    losses = log_total - jnp.sum(jnp.where(one_hot, logits, 0.0), axis=1)
    share = q_rows // owner_count
    loss_share = lax.dynamic_slice_in_dim(losses, owner_index * share, share)
    weighting = (loss_weight * factor)[:, None]
    soft_grad = (
        weighting * (jnp.exp(logits - log_total[:, None]) - one_hot.astype(jnp.float32))
    ).astype(jnp.bfloat16)
    hard_grad = (weighting * jnp.exp(hard_logits - log_total[:, None])).astype(jnp.bfloat16)
    mixing = jnp.sum(jnp.where(picks, hard_grad.astype(jnp.float32)[:, :, None], 0.0), axis=1)
    mix_hi, mix_lo = hi_lo(mixing)
    left = jnp.concatenate([soft_grad, mix_hi, mix_lo], axis=1)
    right = jnp.concatenate([all_passages, table_cols, table_cols], axis=0)
    query_grad = jnp.dot(left, right, preferred_element_type=jnp.float32)
    soft_cols = lax.all_to_all(soft_grad, "blk", split_axis=1, concat_axis=0, tiled=True)
    passage_grad = lax.dot_general(
        soft_cols, all_queries, (((0,), (0,)), ((), ())), preferred_element_type=jnp.float32
    )
    all_hard = lax.all_gather(hard_grad, "blk", axis=0, tiled=True)
    per_col = blk_count // owner_count
    piece_width = col_width // per_col
    shard = blk_index // per_col
    part = blk_index % per_col
    shard_iota = shard * rows_shard + jnp.arange(rows_shard, dtype=jnp.int32)
    shard_picks = all_ids[:, :, None] == shard_iota[None, None, :]
    shard_mix = jnp.sum(
        jnp.where(shard_picks, all_hard.astype(jnp.float32)[:, :, None], 0.0), axis=1
    )
    shard_hi, shard_lo = hi_lo(shard_mix)
    query_part = lax.dynamic_slice_in_dim(all_queries, part * piece_width, piece_width, axis=1)
    dims = (((0,), (0,)), ((), ()))
    piece = lax.dot_general(
        shard_hi, query_part, dims, preferred_element_type=jnp.float32
    ) + lax.dot_general(shard_lo, query_part, dims, preferred_element_type=jnp.float32)
    perm = []
    for b in range(blk_count):
        for c in range(owner_count):
            dest_b = c * per_col + b % per_col
            dest_c = b // per_col
            perm.append((b * owner_count + c, dest_b * owner_count + dest_c))
    table_grad = lax.ppermute(piece, ("blk", "corpus"), perm)
    return (loss_share, query_grad, passage_grad, table_grad)


def solution(mesh):
    placed = (
        P("blk", "corpus"),
        P("blk", "corpus"),
        P("corpus", None),
        P("blk", None),
        P("blk", None),
        P("blk"),
        P("blk"),
    )
    return jax.shard_map(
        per_device,
        mesh=mesh,
        in_specs=placed,
        out_specs=(
            P(("blk", "corpus")),
            P("blk", "corpus"),
            P("blk", "corpus"),
            P("corpus", "blk"),
        ),
        check_vma=False,
    )
```

profile of v0, /device:TPU:2, one launch (start us, length us, event | category | flops | bytes accessed | tf_op | source)
XLA Modules:
  0.0 190.5 jit_solution(2006193391956256831)
XLA Ops:
  7.2 0.7 all-gather.3.cloned.1.call-update
  7.9 3.3 %copy.26 = bf16[256,4096]{0,1:T(8,128)(2,1)S(1)} copy(bf16[256,4096]{1,0:T(8,128)(2,1)} %param.9) | data formatting | bytes 4194304 | tf_op args[2]
  11.2 2.5 %copy.27 = bf16[256,4,1024]{2,0,1:T(8,128)(2,1)} copy(bf16[256,4,1024]{0,2,1:T(8,128)(2,1)S(1)} %bitcast.20) | data formatting | bytes 4194304 | tf_op jit(solution)/shard_map/all_to_all | solution.py:22
  13.7 3.7 %all-to-all-start = ((bf16[256,4,1024]{2,0,1:T(8,128)(2,1)}), bf16[256,4,1024]{2,0,1:T(8,128)(2,1)S(1)}, u32[]{:S(2)}, u32[]{:S(2)}) async-start(bf16[256,4,1024]{2,0,1:T(8,128)(2,1)} %copy.27), calls=%async_computation | async-start | bytes 4194304 | tf_op jit(solution)/shard_map/all_to_all | solution.py:22
  17.5 42.9 %all-gather.3.cloned.1.call-done = bf16[1024,1024]{1,0:T(8,128)(2,1)} async-done(((bf16[128,1024]{1,0:T(8,128)(2,1)}), bf16[1024,1024]{1,0:T(8,128)(2,1)}) %all-gather.3.cloned.1.call-update) | async-done | bytes 2097168 | tf_op jit(solution)/shard_map/all_gather | solution.py:23
  60.5 3.2 %fusion.21 = f32[128,1024]{1,0:T(8,128)} fusion(bf16[128,1024]{1,0:T(8,128)(2,1)S(1)} %copy-done.2, bf16[1024,1024]{1,0:T(8,128)(2,1)} %all-gather.3.cloned.1.call-done), kind=kOutput, calls=%fused_computation.41 | convolution fusion | flops 268435456 | bytes 2883584 | tf_op jit(solution)/shard_map/dot_general | solution.py:28
  64.5 30.6 %all_gather.14 = s32[1024,7]{0,1:T(8,128)S(1)} all-gather(s32[128,7]{0,1:T(8,128)S(1)} %multiply_add_fusion), channel_id=1, replica_groups=mesh['blk'=8,'corpus'=4] {'blk'}, dimensions={0}, use_global_device_ids=true | all-gather | bytes 32256 | tf_op jit(solution)/shard_map/all_gather | solution.py:26
  95.1 0.8 fusion.22
  96.6 5.9 %psum.15 = f32[128,7]{0,1:T(8,128)S(1)} all-reduce(f32[128,7]{0,1:T(8,128)S(1)} %select_reduce_fusion.2), channel_id=1, replica_groups=mesh['blk'=8,'corpus'=4] {'corpus'}, use_global_device_ids=true, to_apply=%region_3.4 | all-reduce | flops 896 | bytes 7168 | tf_op jit(solution)/shard_map/psum | solution.py:37
  102.5 1.2 multiply_reduce_fusion
  103.7 1.4 select_reduce_fusion.3
  105.1 2.1 %copy_bitcast_fusion = bf16[128,8,128]{2,0,1:T(8,128)(2,1)} fusion(s32[128]{0:T(128)S(1)} %copy-done.7, f32[128]{0:T(128)S(1)} %get-tuple-element.11, f32[128,1024]{1,0:T(8,128)} %all-reduce.2.cloned.1.call-done, f32[128]{0:T(128)S(1)} %broadcast_multiply_fusion), kind=kLoop, calls=%fused_computation.26 | loop fusion | flops 917504 | bytes 787968 | tf_op jit(solution)/shard_map/all_to_all | solution.py:59
  107.2 3.4 %all-to-all-start.1 = ((bf16[128,8,128]{2,0,1:T(8,128)(2,1)}), bf16[128,8,128]{2,0,1:T(8,128)(2,1)S(1)}, u32[]{:S(2)}, u32[]{:S(2)}) async-start(bf16[128,8,128]{2,0,1:T(8,128)(2,1)} %copy_bitcast_fusion), calls=%async_computation.1 | async-start | bytes 524288 | tf_op jit(solution)/shard_map/all_to_all | solution.py:59
  110.6 33.2 %all_gather.15 = bf16[1024,7]{0,1:T(8,128)(2,1)S(1)} all-gather(bf16[128,7]{0,1:T(8,128)(2,1)S(1)} %get-tuple-element.9), channel_id=1, replica_groups=mesh['blk'=8,'corpus'=4] {'blk'}, dimensions={0}, use_global_device_ids=true | all-gather | bytes 16128 | tf_op jit(solution)/shard_map/all_gather | solution.py:63
  144.3 0.9 subtract_convert_fusion.2
  145.2 2.5 %select_reduce_fusion = f32[1024,256]{1,0:T(8,128)S(1)} fusion(f32[1024,7]{0,1:T(8,128)S(1)} %convert_element_type.40, s32[256]{0:T(256)S(1)} %iota_add_fusion, s32[1024,7]{0,1:T(8,128)S(1)} %all_gather.14), kind=kLoop, calls=%fused_computation | loop fusion | flops 5242880 | bytes 1106944 | tf_op jit(solution)/shard_map/reduce_sum | solution.py:70
  147.7 3.9 %all-gather.5.cloned.1.call-done = bf16[1024,1024]{1,0:T(8,128)(2,1)} async-done(((bf16[128,1024]{1,0:T(8,128)(2,1)}), bf16[1024,1024]{1,0:T(8,128)(2,1)}) %all-gather.5.cloned.1.call-update) | async-done | bytes 2097168 | tf_op jit(solution)/shard_map/all_gather | solution.py:24
  151.7 1.8 fusion.7
  153.6 1.3 convolution_add_fusion
  154.9 3.7 %collective-permute-start = (f32[256,512]{1,0:T(8,128)}, f32[256,512]{1,0:T(8,128)S(1)}, u32[]{:S(2)}, u32[]{:S(2)}) collective-permute-start(f32[256,512]{1,0:T(8,128)} %convolution_add_fusion), channel_id=1, source_target_pairs={{0,0},{1,8},{2,16},{3,24},{4,4},{5,12},{6,20},{7,28},{8,1},{9,9},{... | collective-permute-start | bytes 1572872 | tf_op jit(solution)/shard_map/ppermute | solution.py:85
  159.0 1.8 fusion
  161.4 2.9 %fusion.23 = f32[128,1024]{1,0:T(8,128)} fusion(bf16[1024,128]{1,0:T(8,128)(2,1)S(1)} %bitcast.21, bf16[1024,1024]{1,0:T(8,128)(2,1)} %all-gather.5.cloned.1.call-done), kind=kOutput, calls=%fused_computation.43 | convolution fusion | flops 268435456 | bytes 2883584 | tf_op jit(solution)/shard_map/dot_general | solution.py:60
  164.2 19.0 %collective-permute-done = f32[256,512]{1,0:T(8,128)S(1)} collective-permute-done((f32[256,512]{1,0:T(8,128)}, f32[256,512]{1,0:T(8,128)S(1)}, u32[]{:S(2)}, u32[]{:S(2)}) %collective-permute-start) | collective-permute-done | bytes 524320 | tf_op jit(solution)/shard_map/ppermute | solution.py:85
  183.2 0.8 copy.33
  (43 shorter events, 3.0 us)
Async XLA Ops:
  7.2 53.3 %all-gather.3.cloned.1.call-start = ((), (), s32[]{:S(2)}) async-start(), calls=%async_computation.2 | async-start | bytes 2359296 | tf_op jit(solution)/shard_map/all_gather | solution.py:23
  13.7 46.8 %copy-start.2 = (bf16[128,1024]{1,0:T(8,128)(2,1)S(1)}, bf16[128,1024]{1,0:T(8,128)(2,1)}, u32[]{:S(2)}) copy-start(bf16[128,1024]{1,0:T(8,128)(2,1)} %param.7) | copy-start | bytes 786436
  13.7 81.4 %all-to-all-start = ((bf16[256,4,1024]{2,0,1:T(8,128)(2,1)}), bf16[256,4,1024]{2,0,1:T(8,128)(2,1)S(1)}, u32[]{:S(2)}, u32[]{:S(2)}) async-start(bf16[256,4,1024]{2,0,1:T(8,128)(2,1)} %copy.27), calls=%async_computation | async-start | bytes 4194304 | tf_op jit(solution)/shard_map/all_to_all | solution.py:22
  17.4 47.0 %copy-start.8 = (s32[128,7]{0,1:T(8,128)S(1)}, s32[128,7]{0,1:T(8,128)}, u32[]{:S(2)}) copy-start(s32[128,7]{0,1:T(8,128)} %param.11) | copy-start | bytes 10756
  17.4 47.0 %copy-start.9 = (s32[128,7]{0,1:T(8,128)S(1)}, s32[128,7]{0,1:T(8,128)}, u32[]{:S(2)}) copy-start(s32[128,7]{0,1:T(8,128)} %param.10) | copy-start | bytes 10756
  17.5 77.7 %copy-start.10 = (f32[128]{0:T(128)S(1)}, f32[128]{0:T(128)}, u32[]{:S(2)}) copy-start(f32[128]{0:T(128)} %param.13) | copy-start | bytes 1540
  17.5 77.7 %copy-start.3 = (bf16[128,1024]{1,0:T(8,128)(2,1)S(1)}, bf16[128,1024]{1,0:T(8,128)(2,1)}, u32[]{:S(2)}) copy-start(bf16[128,1024]{1,0:T(8,128)(2,1)} %param.7) | copy-start | bytes 786436
  17.5 85.1 %all-reduce.2.cloned.1.call-start = ((), (), s32[]{:S(2)}) async-start(), calls=%async_computation.3 | async-start | bytes 1048576 | tf_op jit(solution)/shard_map/psum | solution.py:37
  63.7 88.0 %all-gather.5.cloned.1.call-start = ((), (), s32[]{:S(2)}) async-start(), calls=%async_computation.4 | async-start | bytes 2359296 | tf_op jit(solution)/shard_map/all_gather | solution.py:24
  64.4 39.3 %copy-start.7 = (s32[128]{0:T(128)S(1)}, s32[128]{0:T(128)}, u32[]{:S(2)}) copy-start(s32[128]{0:T(128)} %param.12) | copy-start | bytes 1540
  107.2 54.2 %all-to-all-start.1 = ((bf16[128,8,128]{2,0,1:T(8,128)(2,1)}), bf16[128,8,128]{2,0,1:T(8,128)(2,1)S(1)}, u32[]{:S(2)}, u32[]{:S(2)}) async-start(bf16[128,8,128]{2,0,1:T(8,128)(2,1)} %copy_bitcast_fusion), calls=%async_computation.1 | async-start | bytes 524288 | tf_op jit(solution)/shard_map/all_to_all | solution.py:59
  151.7 1.9 %copy-start = (bf16[1024,1024]{1,0:T(8,128)(2,1)S(1)}, bf16[1024,1024]{1,0:T(8,128)(2,1)}, u32[]{:S(2)}) copy-start(bf16[1024,1024]{1,0:T(8,128)(2,1)} %all-gather.5.cloned.1.call-done) | copy-start | bytes 6291460
  153.6 5.0 %copy-start.1 = (f32[128,1024]{1,0:T(8,128)S(1)}, f32[128,1024]{1,0:T(8,128)}, u32[]{:S(2)}) copy-start(f32[128,1024]{1,0:T(8,128)} %all-reduce.2.cloned.1.call-done) | copy-start | bytes 1572868
  153.6 5.3 %copy-start.4 = (bf16[1024,1024]{1,0:T(8,128)(2,1)S(1)}, bf16[1024,1024]{1,0:T(8,128)(2,1)}, u32[]{:S(2)}) copy-start(bf16[1024,1024]{1,0:T(8,128)(2,1)} %all-gather.3.cloned.1.call-done) | copy-start | bytes 6291460
  153.6 5.3 %copy-start.5 = (bf16[128,1024]{1,0:T(8,128)(2,1)S(1)}, bf16[128,1024]{1,0:T(8,128)(2,1)}, u32[]{:S(2)}) copy-start(bf16[128,1024]{1,0:T(8,128)(2,1)} %get-tuple-element.6) | copy-start | bytes 786436
  153.6 5.4 %copy-start.6 = (bf16[128,1024]{1,0:T(8,128)(2,1)S(1)}, bf16[128,1024]{1,0:T(8,128)(2,1)}, u32[]{:S(2)}) copy-start(bf16[128,1024]{1,0:T(8,128)(2,1)} %get-tuple-element.7) | copy-start | bytes 786436
  154.9 28.3 %collective-permute-start = (f32[256,512]{1,0:T(8,128)}, f32[256,512]{1,0:T(8,128)S(1)}, u32[]{:S(2)}, u32[]{:S(2)}) collective-permute-start(f32[256,512]{1,0:T(8,128)} %convolution_add_fusion), channel_id=1, source_target_pairs={{0,0},{1,8},{2,16},{3,24},{4,4},{5,12},{6,20},{7,28},{8,1},{9,9},{... | collective-permute-start | bytes 1572872 | tf_op jit(solution)/shard_map/ppermute | solution.py:85
Sparse Core Ops, SparseCore 0:
  10.1 50.3 all-gather.2
  63.8 30.5 all-reduce.1
  96.6 55.0 all-gather.4
where the time goes:
time: 191 us
  blocking collectives  69.8 us (37%)
  waiting for transfers between devices  67.3 us (35%)
  between operations  14 us (7%)
  matrix products  11.8 us (6%)
  starting transfers between devices  11 us (6%)
  other arithmetic  9.43 us (5%)
  local copies, waits for them, and re-layouts  7.28 us (4%)
    all_gather x1, waiting for transfers between devices, per_device(): all_passages = lax.all_gather(passages, 'blk', axis=0, tiled=True)  42.9 us
    all_gather x1, blocking collectives, per_device(): all_hard = lax.all_gather(hard_grad, 'blk', axis=0, tiled=True)  33.2 us
    all_gather x1, blocking collectives, per_device(): all_ids = lax.all_gather(ids, 'blk', axis=0, tiled=True)  30.6 us
    ppermute x1, waiting for transfers between devices, per_device(): table_grad = lax.ppermute(piece, ('blk', 'corpus'), perm)  19 us
    psum x1, blocking collectives, per_device(): logits, hard_logits = lax.psum((logits, hard_logits), 'corpus')  5.93 us
    unnamed x24, local copies, waits for them, and re-layouts  4.18 us
    all_gather x1, waiting for transfers between devices, per_device(): all_queries = lax.all_gather(queries, 'blk', axis=0, tiled=True)  3.95 us
  transfers between devices with their start and end apart: 6, of which 3 were waited for; matrix products, arithmetic and copies ran while one was open for 14% of the time, Pallas kernels for 0%

commit v1 on v0

--- a/solution.py
+++ b/solution.py
@@ -2,6 +2,23 @@
 import jax.numpy as jnp
 from jax import lax
 from jax.sharding import PartitionSpec as P
+
+
+def joined_along(pieces, dim):
+    shape = list(pieces.shape[1:])
+    shape[dim] *= pieces.shape[0]
+    return jnp.moveaxis(pieces, 0, dim).reshape(shape)
+
+
+def gather_around(value, axis, dim):
+    size = lax.axis_size(axis)
+    upward = [(i, (i + 1) % size) for i in range(size)]
+    pieces = [value]
+    while len(pieces) < size:
+        pieces.append(lax.ppermute(pieces[-1], axis, upward))
+    index = lax.axis_index(axis)
+    pieces = jnp.stack(pieces)[(index - jnp.arange(size)) % size]
+    return joined_along(pieces, dim)
 
 
 def hi_lo(mixing):
@@ -21,7 +38,7 @@
     blk_index = lax.axis_index("blk")
     table_cols = lax.all_to_all(table, "corpus", split_axis=1, concat_axis=0, tiled=True)
     all_passages = lax.all_gather(passages, "blk", axis=0, tiled=True)
-    all_queries = lax.all_gather(queries, "blk", axis=0, tiled=True)
+    all_queries = gather_around(queries, "blk", 0)
     ids = neg_owner * rows_shard + neg_row
     all_ids = lax.all_gather(ids, "blk", axis=0, tiled=True)
     all_rows = all_passages.shape[0]

time: 191 us -> 229 us (1.20)
  waiting for transfers between devices: 67.3 us -> 92.1 us
  local copies, waits for them, and re-layouts: 7.28 us -> 16.1 us
  starting transfers between devices: 11 us -> 16 us
  blocking collectives: 69.8 us -> 73.9 us
  matrix products: 11.8 us -> 8.85 us
    ppermute x0 -> x7, waiting for transfers between devices: none -> 44.5 us  [gather_around(): pieces.append(lax.ppermute(pieces[-1], axis, upward))]
    all_gather x1, waiting for transfers between devices: 42.9 us -> 0.01 us  [per_device(): all_passages = lax.all_gather(passages, 'blk', axis=0, tiled=True)]
    psum x1, waiting for transfers between devices: 0.01 us -> 30.5 us  [per_device(): logits, hard_logits = lax.psum((logits, hard_logits), 'corpus')]
    all_gather x1, blocking collectives: 30.6 us -> 40.2 us  [per_device(): all_ids = lax.all_gather(ids, 'blk', axis=0, tiled=True)]
    all_gather x1, blocking collectives: 33.2 us -> 27.9 us  [per_device(): all_hard = lax.all_gather(hard_grad, 'blk', axis=0, tiled=True)]
    unnamed x24 -> x29, local copies, waits for them, and re-layouts: 4.18 us -> 9.18 us
    all_gather x1 -> x0, waiting for transfers between devices: 3.95 us -> none  [per_device(): all_queries = lax.all_gather(queries, 'blk', axis=0, tiled=True)]
    ppermute x0 -> x7, starting transfers between devices: none -> 3.15 us  [gather_around(): pieces.append(lax.ppermute(pieces[-1], axis, upward))]
  transfers between devices with their start and end apart: 6 -> 12, of which waited for: 3 -> 6; matrix products, arithmetic and copies ran while one was open for 14% -> 12% of each run, Pallas kernels for 0% -> 0%
where the time goes in v1:
time: 229 us
  waiting for transfers between devices  92.1 us (40%)
  blocking collectives  73.9 us (32%)
  local copies, waits for them, and re-layouts  16.1 us (7%)
  starting transfers between devices  16 us (7%)
  between operations  14.2 us (6%)
  matrix products  8.85 us (4%)
  other arithmetic  7.38 us (3%)
    ppermute x7, waiting for transfers between devices, gather_around(): pieces.append(lax.ppermute(pieces[-1], axis, upward))  44.5 us
    all_gather x1, blocking collectives, per_device(): all_ids = lax.all_gather(ids, 'blk', axis=0, tiled=True)  40.2 us
    psum x1, waiting for transfers between devices, per_device(): logits, hard_logits = lax.psum((logits, hard_logits), 'corpus')  30.5 us
    all_gather x1, blocking collectives, per_device(): all_hard = lax.all_gather(hard_grad, 'blk', axis=0, tiled=True)  27.9 us
    ppermute x1, waiting for transfers between devices, per_device(): table_grad = lax.ppermute(piece, ('blk', 'corpus'), perm)  16.3 us
    unnamed x29, local copies, waits for them, and re-layouts  9.18 us
    all_to_all x1, starting transfers between devices, per_device(): lax.all_to_all(soft_grad, 'blk', split_axis=1, concat_axis=0, tiled=True)  6.06 us
    psum x1, blocking collectives, per_device(): logits, hard_logits = lax.psum((logits, hard_logits), 'corpus')  5.79 us
  transfers between devices with their start and end apart: 12, of which 6 were waited for; matrix products, arithmetic and copies ran while one was open for 12% of the time, Pallas kernels for 0%

profile of v1, /device:TPU:2, one launch (start us, length us, event | category | flops | bytes accessed | tf_op | source)
XLA Modules:
  0.0 228.6 jit_solution(12053792682658917365)
XLA Ops:
  7.9 1.6 collective-permute-start
  9.5 3.3 %copy.23 = bf16[256,4096]{0,1:T(8,128)(2,1)S(1)} copy(bf16[256,4096]{1,0:T(8,128)(2,1)} %param.9) | data formatting | bytes 4194304 | tf_op args[2]
  12.7 2.5 %copy.24 = bf16[256,4,1024]{2,0,1:T(8,128)(2,1)} copy(bf16[256,4,1024]{0,2,1:T(8,128)(2,1)S(1)} %bitcast.38) | data formatting | bytes 4194304 | tf_op jit(solution)/shard_map/all_to_all | solution.py:39
  15.2 4.3 %all-to-all-start = ((bf16[256,4,1024]{2,0,1:T(8,128)(2,1)}), bf16[256,4,1024]{2,0,1:T(8,128)(2,1)S(1)}, u32[]{:S(2)}, u32[]{:S(2)}) async-start(bf16[256,4,1024]{2,0,1:T(8,128)(2,1)} %copy.24), calls=%async_computation | async-start | bytes 4194304 | tf_op jit(solution)/shard_map/all_to_all | solution.py:39
  19.5 1.6 collective-permute-start.1
  21.1 15.4 %collective-permute-done.1 = bf16[128,1024]{1,0:T(8,128)(2,1)S(1)} collective-permute-done((bf16[128,1024]{1,0:T(8,128)(2,1)S(1)}, bf16[128,1024]{1,0:T(8,128)(2,1)S(1)}, u32[]{:S(2)}, u32[]{:S(2)}) %collective-permute-start.1) | collective-permute-done | bytes 262176 | tf_op jit(solution)/shard_map/ppermute | solution.py:18
  37.3 9.6 %collective-permute-done.2 = bf16[128,1024]{1,0:T(8,128)(2,1)S(1)} collective-permute-done((bf16[128,1024]{1,0:T(8,128)(2,1)S(1)}, bf16[128,1024]{1,0:T(8,128)(2,1)S(1)}, u32[]{:S(2)}, u32[]{:S(2)}) %collective-permute-start.2) | collective-permute-done | bytes 262176 | tf_op jit(solution)/shard_map/ppermute | solution.py:18
  46.9 40.2 %all_gather.10 = s32[1024,7]{0,1:T(8,128)S(1)} all-gather(s32[128,7]{0,1:T(8,128)S(1)} %multiply_add_fusion), channel_id=1, replica_groups=mesh['blk'=8,'corpus'=4] {'blk'}, dimensions={0}, use_global_device_ids=true | all-gather | bytes 32256 | tf_op jit(solution)/shard_map/all_gather | solution.py:43
  89.2 10.2 %collective-permute-done.4 = bf16[128,1024]{1,0:T(8,128)(2,1)S(1)} collective-permute-done((bf16[128,1024]{1,0:T(8,128)(2,1)S(1)}, bf16[128,1024]{1,0:T(8,128)(2,1)S(1)}, u32[]{:S(2)}, u32[]{:S(2)}) %collective-permute-start.4) | collective-permute-done | bytes 262176 | tf_op jit(solution)/shard_map/ppermute | solution.py:18
  100.9 9.3 %collective-permute-done.5 = bf16[128,1024]{1,0:T(8,128)(2,1)S(1)} collective-permute-done((bf16[128,1024]{1,0:T(8,128)(2,1)S(1)}, bf16[128,1024]{1,0:T(8,128)(2,1)S(1)}, u32[]{:S(2)}, u32[]{:S(2)}) %collective-permute-start.5) | collective-permute-done | bytes 262176 | tf_op jit(solution)/shard_map/ppermute | solution.py:18
  111.7 5.8 %psum.15 = f32[128,7]{0,1:T(8,128)S(1)} all-reduce(f32[128,7]{0,1:T(8,128)S(1)} %select_reduce_fusion.2), channel_id=1, replica_groups=mesh['blk'=8,'corpus'=4] {'corpus'}, use_global_device_ids=true, to_apply=%region_3.4 | all-reduce | flops 896 | bytes 7168 | tf_op jit(solution)/shard_map/psum | solution.py:54
  118.2 3.2 %fusion.24 = f32[128,1024]{1,0:T(8,128)} fusion(bf16[128,1024]{1,0:T(8,128)(2,1)S(1)} %copy-done.3, bf16[1024,1024]{1,0:T(8,128)(2,1)} %all-gather.2.cloned.1.call-done), kind=kOutput, calls=%fused_computation.58 | convolution fusion | flops 268435456 | bytes 2883584 | tf_op jit(solution)/shard_map/dot_general | solution.py:45
  122.2 2.3 gather_fusion
  124.5 30.5 %all-reduce.2.cloned.1.call-done = f32[128,1024]{1,0:T(8,128)} async-done(((f32[128,1024]{1,0:T(8,128)}), f32[128,1024]{1,0:T(8,128)}) %all-reduce.2.cloned.1.call-update) | async-done | bytes 524304 | tf_op jit(solution)/shard_map/psum | solution.py:54
  155.1 1.2 multiply_reduce_fusion
  156.3 1.4 select_reduce_fusion.3
  160.1 6.1 %all-to-all-start.1 = ((bf16[128,8,128]{0,2,1:T(8,128)(2,1)}), bf16[128,8,128]{0,2,1:T(8,128)(2,1)S(1)}, u32[]{:S(2)}, u32[]{:S(2)}) async-start(bf16[128,8,128]{0,2,1:T(8,128)(2,1)} %bitcast.4), calls=%async_computation.1 | async-start | bytes 524288 | tf_op jit(solution)/shard_map/all_to_all | solution.py:76
  166.2 27.9 %all_gather.11 = bf16[1024,7]{0,1:T(8,128)(2,1)S(1)} all-gather(bf16[128,7]{0,1:T(8,128)(2,1)S(1)} %get-tuple-element.9), channel_id=1, replica_groups=mesh['blk'=8,'corpus'=4] {'blk'}, dimensions={0}, use_global_device_ids=true | all-gather | bytes 16128 | tf_op jit(solution)/shard_map/all_gather | solution.py:80
  194.1 2.5 %select_reduce_fusion = f32[1024,256]{1,0:T(8,128)S(1)} fusion(f32[1024,7]{0,1:T(8,128)S(1)} %convert_element_type.40, s32[256]{0:T(256)S(1)} %iota_add_fusion, s32[1024,7]{0,1:T(8,128)S(1)} %all_gather.10), kind=kLoop, calls=%fused_computation.1 | loop fusion | flops 5242880 | bytes 1106944 | tf_op jit(solution)/shard_map/reduce_sum | solution.py:87
  197.1 1.3 convolution_add_fusion
  198.4 2.5 %collective-permute-start.7 = (f32[256,512]{1,0:T(8,128)}, f32[256,512]{1,0:T(8,128)S(1)}, u32[]{:S(2)}, u32[]{:S(2)}) collective-permute-start(f32[256,512]{1,0:T(8,128)} %convolution_add_fusion), channel_id=1, source_target_pairs={{0,0},{1,8},{2,16},{3,24},{4,4},{5,12},{6,20},{7,28},{8,1},{9,9},{... | collective-permute-start | bytes 1572872 | tf_op jit(solution)/shard_map/ppermute | solution.py:102
  201.6 1.8 fusion
  203.4 1.2 convolution_bitcast_fusion
  204.6 16.3 %collective-permute-done.7 = f32[256,512]{1,0:T(8,128)S(1)} collective-permute-done((f32[256,512]{1,0:T(8,128)}, f32[256,512]{1,0:T(8,128)S(1)}, u32[]{:S(2)}, u32[]{:S(2)}) %collective-permute-start.7) | collective-permute-done | bytes 524320 | tf_op jit(solution)/shard_map/ppermute | solution.py:102
  (63 shorter events, 12.4 us)
Async XLA Ops:
  7.2 111.0 %all-gather.2.cloned.1.call-start = ((), (), s32[]{:S(2)}) async-start(), calls=%async_computation.2 | async-start | bytes 2359296 | tf_op jit(solution)/shard_map/all_gather | solution.py:40
  7.9 11.6 %collective-permute-start = (bf16[128,1024]{1,0:T(8,128)(2,1)}, bf16[128,1024]{1,0:T(8,128)(2,1)S(1)}, u32[]{:S(2)}, u32[]{:S(2)}) collective-permute-start(bf16[128,1024]{1,0:T(8,128)(2,1)} %param.7), channel_id=1, source_target_pairs={{0,4},{4,8},{8,12},{12,16},{16,20},{20,24},{24,28},{28,0},{1,5},{5... | collective-permute-start | bytes 786440 | tf_op jit(solution)/shard_map/ppermute | solution.py:18
  15.2 4.3 %copy-start.9 = (f32[128]{0:T(128)S(1)}, f32[128]{0:T(128)}, u32[]{:S(2)}) copy-start(f32[128]{0:T(128)} %param.13) | copy-start | bytes 1540
  15.2 5.9 %copy-start.6 = (s32[128,7]{0,1:T(8,128)S(1)}, s32[128,7]{0,1:T(8,128)}, u32[]{:S(2)}) copy-start(s32[128,7]{0,1:T(8,128)} %param.11) | copy-start | bytes 10756
  15.2 5.9 %copy-start.7 = (s32[128,7]{0,1:T(8,128)S(1)}, s32[128,7]{0,1:T(8,128)}, u32[]{:S(2)}) copy-start(s32[128,7]{0,1:T(8,128)} %param.10) | copy-start | bytes 10756
  15.2 21.4 %copy-start.3 = (bf16[128,1024]{1,0:T(8,128)(2,1)S(1)}, bf16[128,1024]{1,0:T(8,128)(2,1)}, u32[]{:S(2)}) copy-start(bf16[128,1024]{1,0:T(8,128)(2,1)} %param.7) | copy-start | bytes 786436
  15.2 95.0 %all-to-all-start = ((bf16[256,4,1024]{2,0,1:T(8,128)(2,1)}), bf16[256,4,1024]{2,0,1:T(8,128)(2,1)S(1)}, u32[]{:S(2)}, u32[]{:S(2)}) async-start(bf16[256,4,1024]{2,0,1:T(8,128)(2,1)} %copy.24), calls=%async_computation | async-start | bytes 4194304 | tf_op jit(solution)/shard_map/all_to_all | solution.py:39
  19.5 135.6 %all-reduce.2.cloned.1.call-start = ((), (), s32[]{:S(2)}) async-start(), calls=%async_computation.3 | async-start | bytes 1048576 | tf_op jit(solution)/shard_map/psum | solution.py:54
  19.5 17.0 %collective-permute-start.1 = (bf16[128,1024]{1,0:T(8,128)(2,1)S(1)}, bf16[128,1024]{1,0:T(8,128)(2,1)S(1)}, u32[]{:S(2)}, u32[]{:S(2)}) collective-permute-start(bf16[128,1024]{1,0:T(8,128)(2,1)S(1)} %collective-permute-done), channel_id=1, source_target_pairs={{0,4},{4,8},{8,12},{12,16},{16,20},{20,24},{24,28},{28,0},{1,5},{5... | collective-permute-start | bytes 786440 | tf_op jit(solution)/shard_map/ppermute | solution.py:18
  36.6 10.3 %collective-permute-start.2 = (bf16[128,1024]{1,0:T(8,128)(2,1)S(1)}, bf16[128,1024]{1,0:T(8,128)(2,1)S(1)}, u32[]{:S(2)}, u32[]{:S(2)}) collective-permute-start(bf16[128,1024]{1,0:T(8,128)(2,1)S(1)} %collective-permute-done.1), channel_id=1, source_target_pairs={{0,4},{4,8},{8,12},{12,16},{16,20},{20,24},{24,28},{28,0},{1,5},{5... | collective-permute-start | bytes 786440 | tf_op jit(solution)/shard_map/ppermute | solution.py:18
  46.9 40.9 %collective-permute-start.3 = (bf16[128,1024]{1,0:T(8,128)(2,1)S(1)}, bf16[128,1024]{1,0:T(8,128)(2,1)S(1)}, u32[]{:S(2)}, u32[]{:S(2)}) collective-permute-start(bf16[128,1024]{1,0:T(8,128)(2,1)S(1)} %collective-permute-done.2), channel_id=1, source_target_pairs={{0,4},{4,8},{8,12},{12,16},{16,20},{20,24},{24,28},{28,0},{1,5},{5... | collective-permute-start | bytes 786440 | tf_op jit(solution)/shard_map/ppermute | solution.py:18
  87.8 11.6 %collective-permute-start.4 = (bf16[128,1024]{1,0:T(8,128)(2,1)S(1)}, bf16[128,1024]{1,0:T(8,128)(2,1)S(1)}, u32[]{:S(2)}, u32[]{:S(2)}) collective-permute-start(bf16[128,1024]{1,0:T(8,128)(2,1)S(1)} %collective-permute-done.3), channel_id=1, source_target_pairs={{0,4},{4,8},{8,12},{12,16},{16,20},{20,24},{24,28},{28,0},{1,5},{5... | collective-permute-start | bytes 786440 | tf_op jit(solution)/shard_map/ppermute | solution.py:18
  99.5 10.8 %collective-permute-start.5 = (bf16[128,1024]{1,0:T(8,128)(2,1)S(1)}, bf16[128,1024]{1,0:T(8,128)(2,1)S(1)}, u32[]{:S(2)}, u32[]{:S(2)}) collective-permute-start(bf16[128,1024]{1,0:T(8,128)(2,1)S(1)} %collective-permute-done.4), channel_id=1, source_target_pairs={{0,4},{4,8},{8,12},{12,16},{16,20},{20,24},{24,28},{28,0},{1,5},{5... | collective-permute-start | bytes 786440 | tf_op jit(solution)/shard_map/ppermute | solution.py:18
  110.2 11.2 %collective-permute-start.6 = (bf16[128,1024]{1,0:T(8,128)(2,1)S(1)}, bf16[128,1024]{1,0:T(8,128)(2,1)S(1)}, u32[]{:S(2)}, u32[]{:S(2)}) collective-permute-start(bf16[128,1024]{1,0:T(8,128)(2,1)S(1)} %collective-permute-done.5), channel_id=1, source_target_pairs={{0,4},{4,8},{8,12},{12,16},{16,20},{20,24},{24,28},{28,0},{1,5},{5... | collective-permute-start | bytes 786440 | tf_op jit(solution)/shard_map/ppermute | solution.py:18
  110.2 11.2 %copy-start = (bf16[256,4,1024]{2,0,1:T(8,128)(2,1)}, bf16[256,4,1024]{2,0,1:T(8,128)(2,1)S(1)}, u32[]{:S(2)}) copy-start(bf16[256,4,1024]{2,0,1:T(8,128)(2,1)S(1)} %all-to-all-done) | copy-start | bytes 6291460
  122.2 34.1 %copy-start.8 = (s32[128]{0:T(128)S(1)}, s32[128]{0:T(128)}, u32[]{:S(2)}) copy-start(s32[128]{0:T(128)} %param.12) | copy-start | bytes 1540
  155.0 3.9 %copy-start.2 = (f32[128,1024]{1,0:T(8,128)S(1)}, f32[128,1024]{1,0:T(8,128)}, u32[]{:S(2)}) copy-start(f32[128,1024]{1,0:T(8,128)} %all-reduce.2.cloned.1.call-done) | copy-start | bytes 1572868
  160.1 43.3 %all-to-all-start.1 = ((bf16[128,8,128]{0,2,1:T(8,128)(2,1)}), bf16[128,8,128]{0,2,1:T(8,128)(2,1)S(1)}, u32[]{:S(2)}, u32[]{:S(2)}) async-start(bf16[128,8,128]{0,2,1:T(8,128)(2,1)} %bitcast.4), calls=%async_computation.1 | async-start | bytes 524288 | tf_op jit(solution)/shard_map/all_to_all | solution.py:76
  196.6 4.9 %copy-start.4 = (bf16[1024,1024]{1,0:T(8,128)(2,1)S(1)}, bf16[1024,1024]{1,0:T(8,128)(2,1)}, u32[]{:S(2)}) copy-start(bf16[1024,1024]{1,0:T(8,128)(2,1)} %all-gather.2.cloned.1.call-done) | copy-start | bytes 6291460
  197.1 4.4 %copy-start.1 = (bf16[256,4,1024]{2,0,1:T(8,128)(2,1)S(1)}, bf16[256,4,1024]{2,0,1:T(8,128)(2,1)}, u32[]{:S(2)}) copy-start(bf16[256,4,1024]{2,0,1:T(8,128)(2,1)} %copy-done) | copy-start | bytes 6291460
  197.1 4.4 %copy-start.5 = (bf16[128,1024]{1,0:T(8,128)(2,1)S(1)}, bf16[128,1024]{1,0:T(8,128)(2,1)}, u32[]{:S(2)}) copy-start(bf16[128,1024]{1,0:T(8,128)(2,1)} %get-tuple-element.7) | copy-start | bytes 786436
  198.4 22.5 %collective-permute-start.7 = (f32[256,512]{1,0:T(8,128)}, f32[256,512]{1,0:T(8,128)S(1)}, u32[]{:S(2)}, u32[]{:S(2)}) collective-permute-start(f32[256,512]{1,0:T(8,128)} %convolution_add_fusion), channel_id=1, source_target_pairs={{0,0},{1,8},{2,16},{3,24},{4,4},{5,12},{6,20},{7,28},{8,1},{9,9},{... | collective-permute-start | bytes 1572872 | tf_op jit(solution)/shard_map/ppermute | solution.py:102
Sparse Core Ops, SparseCore 0:
  10.1 60.8 all-gather.1
  121.6 33.4 all-reduce.1
